TPU v7x, 256 devices: a whole 4x4x8 slice. The times are simulated.
256 devices in a mesh: frame: 16 (over z_lo, y), tensor: 8 (over z_hi, x), dp: 2 (over core).
Axes of the slice: x: 4, y: 4, z: 8 (z_hi: 2, z_lo: 4; z = z_hi * 4 + z_lo), core: 2. Of those that a mesh axis runs over, the one named last changes fastest.
Arguments:
- q_proj: bfloat16 [16384, 3072], P(('dp', 'frame'), 'tensor'), parts along dimension 0
- k_proj: bfloat16 [16384, 3072], P(('dp', 'frame'), 'tensor'), parts along dimension 0
- v_proj: bfloat16 [16384, 3072], P(('dp', 'frame'), 'tensor'), parts along dimension 0, may hold values from -6 to 6
- gain_q: float32 [3072], P('tensor'), may hold values from 0.5 to 6
- gain_k: float32 [3072], P('tensor'), may hold values from 0.5 to 6
- tiles: int32 [128, 12], P('dp'), parts along dimension 0, may hold values from 0 to 63, as said below
Outputs:
- attended: bfloat16 [16384, 3072], P(('dp', 'frame'), 'tensor'), parts along dimension 0
There are 2 independent parts, one for each index of `dp`. A program takes and returns all parts, laid end to end along the dimension named above; an argument that names none is the same for every part. Nothing has to cross between parts.
Inputs may be any that keep to these rules, and one draw needn't show every extreme that they name: `tiles`: row q lists 12 distinct key blocks: q first; then 8 blocks whose slab (group of 4 consecutive blocks, one frame slab) is at most 2 slabs from the slab of q; then 3 blocks that are each the first block of a slab more than 2 slabs away. Farther groups are listed less often.
All inputs are finite; a program needn't handle non-finite values.
Results may differ from a plain program's by a relative error of at most 0.007.
The roundings to bfloat16 on the way count: a program that leaves them out, or rounds other values in their place, can miss the bound.
Values may be sent and summed in bfloat16 or wider, within the bound.
No kernel may reach another device: no remote copies, remote signals or barrier semaphores. Data moves between devices by JAX's collectives and lax.ppermute only.
A program may use at most 128 MiB of HBM per device.

v0:
```python
import math
import jax
import jax.numpy as jnp
from jax import lax
from jax.sharding import PartitionSpec as P

HD = 128
BLK = 128
EPS = 1e-06


def attend(state_now, q_heads, keys, values, key_ids, q_tiles):
    run_max, run_sum, run_acc = state_now
    head_count = run_max.shape[0]
    tok_rows = q_heads.shape[0]
    length = keys.shape[0]
    k_heads = keys.reshape(length, head_count, HD)
    v_heads = values.reshape(length, head_count, HD)
    scores = jnp.einsum("qhd,khd->hqk", q_heads, k_heads, preferred_element_type=jnp.float32) * (
        1.0 / math.sqrt(HD)
    )
    listed = jnp.any(q_tiles[:, :, None] == key_ids[None, None, :], axis=1)
    listed = jnp.repeat(listed, tok_rows // q_tiles.shape[0], axis=0)[None]
    scores = jnp.where(listed, scores, -1e30)
    new_max = jnp.maximum(run_max, jnp.max(scores, axis=-1))
    factor = jnp.exp(run_max - new_max)
    weights = jnp.where(listed, jnp.exp(scores - new_max[..., None]), 0.0)
    new_sum = run_sum * factor + jnp.sum(weights, axis=-1)
    product = jnp.einsum(
        "hqk,khd->hqd", weights.astype(jnp.bfloat16), v_heads, preferred_element_type=jnp.float32
    )
    new_acc = run_acc * factor[..., None] + product
    return (new_max, new_sum, new_acc)


def sweep(state_now, q_heads, keys, values, key_ids, q_tiles):
    length = keys.shape[0]
    sub_rows = math.gcd(length, 512)
    steps_count = length // sub_rows
    width = keys.shape[1]
    inputs = (
        keys.reshape(steps_count, sub_rows, width),
        values.reshape(steps_count, sub_rows, width),
        key_ids.reshape(steps_count, sub_rows),
    )

    def one_step(carried, parts_now):
        return (attend(carried, q_heads, parts_now[0], parts_now[1], parts_now[2], q_tiles), None)

    final_state, unused = lax.scan(one_step, state_now, inputs)
    return final_state


def body(q_proj, k_proj, v_proj, gain_q, gain_k, tiles):
    tok_rows, width = q_proj.shape
    head_count = width // HD
    q_wide = q_proj.astype(jnp.float32)
    k_wide = k_proj.astype(jnp.float32)
    row_sums = lax.psum(
        (jnp.sum(q_wide * q_wide, axis=1), jnp.sum(k_wide * k_wide, axis=1)), "tensor"
    )
    full_width = width * lax.axis_size("tensor")
    q_norm = (q_wide * lax.rsqrt(row_sums[0] / full_width + EPS)[:, None] * gain_q).astype(
        jnp.bfloat16
    )
    k_norm = (k_wide * lax.rsqrt(row_sums[1] / full_width + EPS)[:, None] * gain_k).astype(
        jnp.bfloat16
    )
    blocks = tok_rows // BLK
    frame_pos = lax.axis_index("frame")
    q_tiles = lax.dynamic_slice_in_dim(tiles, frame_pos * blocks, blocks, 0)
    q_heads = q_norm.reshape(tok_rows, head_count, HD)
    kv_pair = jnp.stack([k_norm, v_proj])
    state_now = (
        jnp.full((head_count, tok_rows), -1e30, jnp.float32),
        jnp.zeros((head_count, tok_rows), jnp.float32),
        jnp.zeros((head_count, tok_rows, HD), jnp.float32),
    )
    portion = lax.all_gather(kv_pair, "frame", axis=1, tiled=True)
    length = portion.shape[1]
    key_ids = jnp.arange(length, dtype=jnp.int32) // BLK
    state_now = sweep(state_now, q_heads, portion[0], portion[1], key_ids, q_tiles)
    run_max, run_sum, run_acc = state_now
    result = run_acc / run_sum[..., None]
    return jnp.transpose(result, (1, 0, 2)).reshape(tok_rows, width).astype(jnp.bfloat16)


def solution(mesh):
    return jax.shard_map(
        body,
        mesh=mesh,
        in_specs=(
            P(("dp", "frame"), "tensor"),
            P(("dp", "frame"), "tensor"),
            P(("dp", "frame"), "tensor"),
            P("tensor"),
            P("tensor"),
            P("dp", None),
        ),
        out_specs=P(("dp", "frame"), "tensor"),
        check_vma=False,
    )
```

profile of v0, /device:TPU:1, one launch (start us, length us, event | category | flops | bytes accessed | tf_op | source)
XLA Modules:
  0.0 416.1 jit_solution(15182845750359665627)
XLA Ops:
  9.0 30.2 %all-reduce = (f32[512]{0:T(512)S(1)}, f32[512]{0:T(512)S(1)}) all-reduce(f32[512]{0:T(512)S(1)} %fusion.13, f32[512]{0:T(512)S(1)} %fusion.16), channel_id=1, replica_groups=mesh['frame'=16,'tensor'=8,'dp'=2] {'tensor'}, use_global_device_ids=true, to_apply=%region_1.0 | all-reduce | flops 1024 | bytes 8192 | tf_op jit(solution)/shard_map/psum | solution.py:59
  40.4 2.0 pad_maximum_fusion
  43.6 142.4 %all-gather.2.cloned.1.call-done = bf16[2,8192,384]{2,1,0:T(8,128)(2,1)} async-done(((bf16[2,512,384]{2,1,0:T(8,128)(2,1)}), bf16[2,8192,384]{2,1,0:T(8,128)(2,1)}) %all-gather.2.cloned.1.call-update) | async-done | bytes 12582928 | tf_op jit(solution)/shard_map/all_gather | solution.py:79
  186.0 10.2 %fusion.23 = (bf16[1,8192,384]{2,1,0:T(8,128)(2,1)}, bf16[1,8192,384]{2,1,0:T(8,128)(2,1)}) fusion(bf16[2,8192,384]{2,1,0:T(8,128)(2,1)} %all-gather.2.cloned.1.call-done), kind=kLoop, calls=%fused_computation.46 | loop fusion | bytes 25165824 | tf_op jit(solution)/shard_map/slice | solution.py:82
  196.2 210.6 %while.15 = (s32[]{:T(128)}, f32[3,512]{1,0:T(4,128)S(1)}, f32[3,512]{1,0:T(4,128)S(1)}, f32[3,512,128]{2,1,0:T(8,128)}, s32[4,12]{0,1:T(8,128)S(1)}, /*index=5*...) while((s32[]{:T(128)}, f32[3,512]{1,0:T(4,128)S(1)}, ...), condition=%wide.region_8.9_spmd.clone, body=%wide.region_4.8_spmd.clone.sunk | while | flops 413521408 | bytes 17021248 | solution.py:50
  205.9 3.2 fusion.42
  218.8 3.5 fusion.42
  232.0 3.5 fusion.42
  245.2 3.5 fusion.42
  253.6 2.0 fusion.39
  258.4 3.5 fusion.42
  271.5 3.5 fusion.42
  280.0 2.0 fusion.39
  284.7 3.5 fusion.42
  297.9 3.5 fusion.42
  311.1 3.5 fusion.42
  324.3 3.5 fusion.42
  332.7 2.0 fusion.39
  337.4 3.5 fusion.42
  350.6 3.5 fusion.42
  363.8 3.5 fusion.42
  377.0 3.5 fusion.42
  390.1 3.5 fusion.42
  403.3 3.5 fusion.42
  (226 shorter events, 155.4 us)
Async XLA Ops:
  6.5 37.0 %copy-start = (s32[64,12]{0,1:T(8,128)S(1)}, s32[64,12]{0,1:T(8,128)}, u32[]{:S(2)}) copy-start(s32[64,12]{0,1:T(8,128)} %param.13) | copy-start | bytes 9220
  6.5 35.9 %copy-start.1 = (f32[384]{0:T(512)S(1)}, f32[384]{0:T(512)}, u32[]{:S(2)}) copy-start(f32[384]{0:T(512)} %param.11) | copy-start | bytes 4612
  6.5 179.4 %all-gather.2.cloned.1.call-start = ((), (), s32[]{:S(2)}) async-start(), calls=%async_computation | async-start | bytes 13369344 | tf_op jit(solution)/shard_map/all_gather | solution.py:79
Sparse Core Ops, SparseCore 0:
  42.5 143.3 all-gather.1
where the time goes:
time: 418 us; the launch traced here: 416 us
  waiting for transfers between devices  142 us (34%)
  local copies, waits for them, and re-layouts  122 us (29%)
  matrix products  87 us (21%)
  blocking collectives  30.2 us (7%)
  other arithmetic  19.6 us (5%)
  between operations  13.5 us (3%)
    all_gather x1, waiting for transfers between devices, body(): portion = lax.all_gather(kv_pair, 'frame', axis=1, tiled=True)  142 us
    dynamic_slice x64, local copies, waits for them, and re-layouts, sweep(): final_state, unused = lax.scan(one_step, state_now, inputs)  76.9 us
    dot_general x16, matrix products, attend(): jnp.einsum('hqk,khd->hqd', weights.astype(jnp.bfloat16), v_heads, preferr...  55.6 us
    dot_general x16, matrix products, attend(): jnp.einsum('qhd,khd->hqk', q_heads, k_heads, preferred_element_type=jnp.f...  31.5 us
    psum x1, blocking collectives, body(): lax.psum((jnp.sum(q_wide * q_wide, axis=1), jnp.sum(k_wide * k_wide, axis...  30.2 us
    broadcast_in_dim x16, local copies, waits for them, and re-layouts, attend(): listed = jnp.repeat(listed, tok_rows // q_tiles.shape[0], axis=0)[None]  25.6 us
    reduce_sum x16, other arithmetic, attend(): new_sum = run_sum * factor + jnp.sum(weights, axis=-1)  12.9 us
    slice x1, local copies, waits for them, and re-layouts, body(): portion[1]  10.2 us
  transfers between devices with their start and end apart: 1, of which 1 were waited for; matrix products, arithmetic and copies ran while one was open for 0% of the time, Pallas kernels for 0%

commit v1 on v0

--- a/solution.py
+++ b/solution.py
@@ -76,7 +76,9 @@
         jnp.zeros((head_count, tok_rows), jnp.float32),
         jnp.zeros((head_count, tok_rows, HD), jnp.float32),
     )
-    portion = lax.all_gather(kv_pair, "frame", axis=1, tiled=True)
+    portion = jnp.concatenate(
+        lax.all_to_all(jnp.stack([kv_pair] * lax.axis_size("frame")), "frame", 0, 0), axis=1
+    )
     length = portion.shape[1]
     key_ids = jnp.arange(length, dtype=jnp.int32) // BLK
     state_now = sweep(state_now, q_heads, portion[0], portion[1], key_ids, q_tiles)

time: 418 us -> 486 us (1.16)
  the two profiles are of different devices: /device:TPU:1 before, /device:TPU:64 now
where the time goes in v1:
time: 486 us; the launch traced here: 484 us
  waiting for transfers between devices  268 us (55%)
  local copies, waits for them, and re-layouts  104 us (21%)
  matrix products  53.1 us (11%)
  blocking collectives  31.3 us (6%)
  other arithmetic  18.7 us (4%)
  starting transfers between devices  7.43 us (2%)
    all_to_all x1, waiting for transfers between devices, body(): lax.all_to_all(jnp.stack([kv_pair] * lax.axis_size('frame')), 'frame', 0, 0)  268 us
    psum x1, blocking collectives, body(): lax.psum((jnp.sum(q_wide * q_wide, axis=1), jnp.sum(k_wide * k_wide, axis...  31.3 us
    dynamic_slice x32, local copies, waits for them, and re-layouts, sweep(): final_state, unused = lax.scan(one_step, state_now, inputs)  30.7 us
    dot_general x16, matrix products, attend(): jnp.einsum('qhd,khd->hqk', q_heads, k_heads, preferred_element_type=jnp.f...  29.6 us
    broadcast_in_dim x16, local copies, waits for them, and re-layouts, attend(): listed = jnp.repeat(listed, tok_rows // q_tiles.shape[0], axis=0)[None]  25.6 us
    dot_general x16, matrix products, attend(): jnp.einsum('hqk,khd->hqd', weights.astype(jnp.bfloat16), v_heads, preferr...  23.6 us
    while x128, local copies, waits for them, and re-layouts  23.3 us
    reduce_sum x16, other arithmetic, attend(): new_sum = run_sum * factor + jnp.sum(weights, axis=-1)  12.9 us
  transfers between devices with their start and end apart: 1, of which 1 were waited for; matrix products, arithmetic and copies ran while one was open for 0% of the time, Pallas kernels for 0%

profile of v1, /device:TPU:64, one launch (start us, length us, event | category | flops | bytes accessed | tf_op | source)
XLA Modules:
  0.0 484.0 jit_solution(1854542131760568816)
XLA Ops:
  2.5 31.3 %all-reduce = (f32[512]{0:T(512)S(1)}, f32[512]{0:T(512)S(1)}) all-reduce(f32[512]{0:T(512)S(1)} %fusion.13, f32[512]{0:T(512)S(1)} %fusion.16), channel_id=1, replica_groups=mesh['frame'=16,'tensor'=8,'dp'=2] {'tensor'}, use_global_device_ids=true, to_apply=%region_1.0 | all-reduce | flops 1024 | bytes 8192 | tf_op jit(solution)/shard_map/psum | solution.py:59
  36.4 5.9 %stack.11 = bf16[16,2,512,384]{2,3,1,0:T(8,128)(2,1)} broadcast(bf16[2,512,384]{1,2,0:T(8,128)(2,1)S(1)} %copy.32), dimensions={1,2,3} | broadcast | bytes 13369344 | tf_op jit(solution)/shard_map/stack | solution.py:80
  42.3 7.4 %all-to-all-start = ((bf16[16,2,512,384]{2,3,1,0:T(8,128)(2,1)}), bf16[16,2,512,384]{2,3,1,0:T(8,128)(2,1)}, u32[]{:S(2)}, u32[]{:S(2)}) async-start(bf16[16,2,512,384]{2,3,1,0:T(8,128)(2,1)} %stack.11), calls=%async_computation | async-start | bytes 25165824 | tf_op jit(solution)/shard_map/all_to_all | solution.py:80
  50.9 268.1 %all-to-all-done = bf16[16,2,512,384]{2,3,1,0:T(8,128)(2,1)} async-done(((bf16[16,2,512,384]{2,3,1,0:T(8,128)(2,1)}), bf16[16,2,512,384]{2,3,1,0:T(8,128)(2,1)}, u32[]{:S(2)}, u32[]{:S(2)}) %all-to-all-start) | async-done | bytes 12582944 | tf_op jit(solution)/shard_map/all_to_all | solution.py:80
  319.0 10.4 %slice_bitcast_fusion = (bf16[16,512,384]{1,2,0:T(8,128)(2,1)}, bf16[16,512,384]{1,2,0:T(8,128)(2,1)}) fusion(bf16[2,16,512,384]{2,3,0,1:T(8,128)(2,1)} %bitcast.2), kind=kLoop, calls=%fused_computation.21 | loop fusion | bytes 25165824 | tf_op jit(solution)/shard_map/reshape;squeeze | solution.py:43
  329.5 152.1 %while.15 = (s32[]{:T(128)}, f32[3,512]{1,0:T(4,128)S(1)}, f32[3,512]{1,0:T(4,128)S(1)}, f32[3,512,128]{2,1,0:T(8,128)}, s32[4,12]{0,1:T(8,128)S(1)}, /*index=5*...) while((s32[]{:T(128)}, f32[3,512]{1,0:T(4,128)S(1)}, ...), condition=%wide.region_8.9_spmd.clone, body=%wide.region_4.8_spmd.clone.sunk | while | flops 413521408 | bytes 23312788 | solution.py:50
  331.5 1.9 constant_dynamic-slice_fusion.7
  341.0 1.9 constant_dynamic-slice_fusion.7
  350.5 1.9 constant_dynamic-slice_fusion.7
  360.0 1.9 constant_dynamic-slice_fusion.7
  361.9 1.9 fusion.38
  369.5 1.9 constant_dynamic-slice_fusion.7
  379.0 1.9 constant_dynamic-slice_fusion.7
  388.5 1.9 constant_dynamic-slice_fusion.7
  398.0 1.9 constant_dynamic-slice_fusion.7
  400.0 1.9 fusion.38
  407.6 1.9 constant_dynamic-slice_fusion.7
  417.1 1.9 constant_dynamic-slice_fusion.7
  426.6 1.9 constant_dynamic-slice_fusion.7
  436.1 1.9 constant_dynamic-slice_fusion.7
  445.6 1.9 constant_dynamic-slice_fusion.7
  455.1 1.9 constant_dynamic-slice_fusion.7
  464.6 1.9 constant_dynamic-slice_fusion.7
  474.1 1.9 constant_dynamic-slice_fusion.7
  (291 shorter events, 125.1 us)
Async XLA Ops:
  0.0 50.8 %copy-start = (s32[64,12]{0,1:T(8,128)S(1)}, s32[64,12]{0,1:T(8,128)}, u32[]{:S(2)}) copy-start(s32[64,12]{0,1:T(8,128)} %param.13) | copy-start | bytes 9220
  42.3 7.5 %copy-start.4 = (f32[384]{0:T(512)S(1)}, f32[384]{0:T(512)}, u32[]{:S(2)}) copy-start(f32[384]{0:T(512)} %param.11) | copy-start | bytes 4612
  42.3 276.8 %all-to-all-start = ((bf16[16,2,512,384]{2,3,1,0:T(8,128)(2,1)}), bf16[16,2,512,384]{2,3,1,0:T(8,128)(2,1)}, u32[]{:S(2)}, u32[]{:S(2)}) async-start(bf16[16,2,512,384]{2,3,1,0:T(8,128)(2,1)} %stack.11), calls=%async_computation | async-start | bytes 25165824 | tf_op jit(solution)/shard_map/all_to_all | solution.py:80
  335.3 1.0 copy-start.1
  335.3 1.2 copy-start.2
  344.8 1.0 copy-start.1
  344.8 1.2 copy-start.2
  354.3 1.0 copy-start.1
  354.3 1.2 copy-start.2
  363.8 1.0 copy-start.1
  363.8 1.2 copy-start.2
  373.3 1.2 copy-start.2
  382.8 1.2 copy-start.2
  392.3 1.2 copy-start.2
  401.8 1.2 copy-start.2
  411.3 1.0 copy-start.1
  411.3 1.2 copy-start.2
  420.8 1.2 copy-start.2
  430.3 1.2 copy-start.2
  439.8 1.2 copy-start.2
  449.4 1.2 copy-start.2
  458.9 1.2 copy-start.2
  468.4 1.2 copy-start.2
  477.9 1.2 copy-start.2
  (27 other events, 26.0 us)
